TPU v7x, 256 devices: a whole 4x4x8 slice. The times are simulated.
256 devices in a mesh: gx: 8 (over x, core), yz: 32 (over z, y).
Axes of the slice: x: 4, y: 4, z: 8, core: 2. Of those that a mesh axis runs over, the one named last changes fastest.
Arguments:
- velocity: float32 [3, 256, 512, 128], P(None, 'gx', 'yz'), may hold values from -6 to 6
- old_pressure: float32 [256, 512, 128], P('gx', 'yz'), may hold values from -3 to 3
- delta_weight: bfloat16 [8, 1024, 128, 128], P('gx', 'yz'), may hold values from -0.5 to 0.5
- marker_target: float32 [8, 1024, 3, 128], P('gx', 'yz'), may hold values from -6 to 6
- pair_owner: int32 [8, 1024, 1], P('gx', 'yz'), may hold values from 0 to 31; in each aligned block of 32 rows (0 to 31, 32 to 63, ..., all dimensions but the last counted through in order) at most 4 rows name the same one
- pair_grain: int32 [8, 1024], P('gx', 'yz'), may hold values from 0 to 31
- box_anchor: int32 [8, 1024, 3], P('gx', 'yz'), may hold values from 0 to 120, as said below
Outputs:
- new_velocity: float32 [3, 256, 512, 128], P(None, 'gx', 'yz')
- pressure: float32 [256, 512, 128], P('gx', 'yz')
Inputs may be any that keep to these rules, and one draw needn't show every extreme that they name: Block r of slab i lies on tile r // 32 of that slab; its grain is owned by tile pair_owner of the same slab. Among the 32 blocks of one tile at most 4 name the same owner, and some tile reaches 4. `pair_grain`: blocks of one slab with equal owner and grain slot belong to one grain. `box_anchor`: column 0 is at most 28, column 1 at most 12, column 2 at most 120, and each of these is reached, so every box lies inside its tile.
All inputs are finite; a program needn't handle non-finite values.
Results may differ from a plain program's by a relative error of at most 0.002.
Values may be sent and summed in bfloat16 or wider, within the bound.
No kernel may reach another device: no remote copies, remote signals or barrier semaphores. Data moves between devices by JAX's collectives and lax.ppermute only.
A program may use at most 128 MiB of HBM per device.

v0:
```python
import jax
import jax.numpy as jnp
from jax import lax
from jax.sharding import PartitionSpec as P

BX = 4
BZ = 4
BY = 8
step_size = 0.1
viscosity = 1.5


def extended(block, sides, width):
    for axis, dim in sides:
        count = lax.axis_size(axis)
        forward = [(i, i + 1) for i in range(count - 1)]
        forward.append((count - 1, 0))
        backward = [(target, source) for source, target in forward]
        low = lax.ppermute(
            lax.slice_in_dim(block, block.shape[dim] - width, None, axis=dim), axis, forward
        )
        high = lax.ppermute(lax.slice_in_dim(block, 0, width, axis=dim), axis, backward)
        block = jnp.concatenate([low, block, high], axis=dim)
    return block


def inner(padded):
    return padded[..., 1:-1, 1:-1, :]


def along_x(padded):
    return 0.5 * (padded[..., 2:, 1:-1, :] - padded[..., :-2, 1:-1, :])


def along_z(padded):
    return 0.5 * (padded[..., 1:-1, 2:, :] - padded[..., 1:-1, :-2, :])


def along_y(field):
    return 0.5 * (jnp.roll(field, -1, -1) - jnp.roll(field, 1, -1))


def neighbours(padded):
    middle = inner(padded)
    total = padded[..., 2:, 1:-1, :] + padded[..., :-2, 1:-1, :]
    total = total + padded[..., 1:-1, 2:, :] + padded[..., 1:-1, :-2, :]
    return total + jnp.roll(middle, 1, -1) + jnp.roll(middle, -1, -1)


def gradient_of(padded):
    middle = inner(padded)
    return jnp.stack([along_x(padded), along_y(middle), along_z(padded)])


def predict(flow_padded):
    velocity_padded = flow_padded[:3]
    pressure_padded = flow_padded[3]
    current = inner(velocity_padded)
    laplace = neighbours(velocity_padded) - 6.0 * current
    advect = current[0] * along_x(velocity_padded)
    return current + step_size * (viscosity * laplace - advect) - gradient_of(pressure_padded)


def kernel_box_cells(anchors, box_x, box_z, box_y):
    steps_x = jnp.arange(box_x, dtype=jnp.int32)
    steps_z = jnp.arange(box_z, dtype=jnp.int32)
    steps_y = jnp.arange(box_y, dtype=jnp.int32)
    cell_x = anchors[:, 0, None, None, None] + steps_x[None, :, None, None]
    cell_z = anchors[:, 1, None, None, None] + steps_z[None, None, :, None]
    cell_y = anchors[:, 2, None, None, None] + steps_y[None, None, None, :]
    return (cell_x, cell_z, cell_y)


def walls(padded, vertical_dim):
    tile_index = lax.axis_index("yz")
    tile_total = lax.axis_size("yz")
    extent = padded.shape[vertical_dim]
    position = lax.broadcasted_iota(jnp.int32, padded.shape, vertical_dim)
    bottom_rim = jnp.logical_and(position == 0, tile_index == 0)
    top_rim = jnp.logical_and(position == extent - 1, tile_index == tile_total - 1)
    return jnp.where(jnp.logical_or(bottom_rim, top_rim), jnp.zeros((), padded.dtype), padded)


def pressure_cycle(pressure):
    padded = extended(pressure, (("gx", 0), ("yz", 1)), 1)
    return walls(padded, 1)


def body(velocity, old_pressure, delta_weight, marker_target, pair_owner, pair_grain, box_anchor):
    flow_fields = jnp.concatenate([velocity, old_pressure[None]], 0)
    flow_padded = walls(extended(flow_fields, (("gx", 1), ("yz", 2)), 1), 2)
    predicted = predict(flow_padded)
    anchors = box_anchor[0]
    owners = pair_owner[0, :, 0]
    grains = pair_grain[0]
    delta_weights = delta_weight[0]
    grain_slots = marker_target.shape[1]
    pair_total = anchors.shape[0]
    cell_x, cell_z, cell_y = kernel_box_cells(anchors, BX, BZ, BY)
    kernel_box_values = (
        predicted[:, cell_x, cell_z, cell_y].astype(jnp.bfloat16).reshape(3, pair_total, -1)
    )
    partial_force_value = jnp.einsum(
        "eky,iey->eik", delta_weights, kernel_box_values, preferred_element_type=jnp.float32
    )
    row_width = partial_force_value.shape[1] * partial_force_value.shape[2]
    flat_partial = partial_force_value.reshape(pair_total, row_width)
    targets = marker_target[0].reshape(grain_slots, row_width)
    slot_numbers = jnp.arange(grain_slots, dtype=jnp.int32)
    all_partial, all_owner, all_grain = (
        lax.all_gather(flat_partial, "yz", axis=0, tiled=True),
        lax.all_gather(owners, "yz", axis=0, tiled=True),
        lax.all_gather(grains, "yz", axis=0, tiled=True),
    )
    own_tile = lax.axis_index("yz")
    grain_keys = jnp.where(all_owner == own_tile, all_grain, grain_slots)
    select = (grain_keys[None, :] == slot_numbers[:, None]).astype(jnp.float32)
    summed = jnp.dot(
        select, all_partial, precision=lax.Precision.HIGHEST, preferred_element_type=jnp.float32
    )
    grain_force = (targets - summed).astype(jnp.bfloat16)
    all_force = lax.all_gather(grain_force, "yz", axis=0, tiled=True)
    marker_pair_force = jnp.take(all_force, owners * grain_slots + grains, axis=0)
    spread_force = jnp.einsum(
        "zwx,znw->nzx",
        delta_weights,
        marker_pair_force.reshape(pair_total, 3, -1),
        preferred_element_type=jnp.float32,
    )
    spread_force = spread_force.reshape(3, pair_total, BX, BZ, BY)
    forced_velocity = predicted + jnp.zeros_like(predicted).at[:, cell_x, cell_z, cell_y].add(
        spread_force
    )
    forced_padded = walls(extended(forced_velocity, (("gx", 1), ("yz", 2)), 1), 2)
    divergence = along_x(forced_padded[0]) + along_y(forced_velocity[1]) + along_z(forced_padded[2])
    first_padded = pressure_cycle(old_pressure)
    pressure = (neighbours(first_padded) - divergence) / 6.0
    pressure = (neighbours(pressure_cycle(pressure)) - divergence) / 6.0
    new_velocity = forced_velocity - gradient_of(pressure_cycle(pressure))
    return (new_velocity, pressure)


def solution(mesh):
    placed = (
        P(None, "gx", "yz", None),
        P("gx", "yz", None),
        P("gx", "yz", None, None),
        P("gx", "yz", None, None),
        P("gx", "yz", None),
        P("gx", "yz"),
        P("gx", "yz", None),
    )
    return jax.shard_map(
        body,
        mesh=mesh,
        in_specs=placed,
        out_specs=(P(None, "gx", "yz", None), P("gx", "yz", None)),
        check_vma=False,
    )
```

profile of v0, /device:TPU:7, one launch (start us, length us, event | category | flops | bytes accessed | tf_op | source)
XLA Modules:
  0.0 358.6 jit_solution(16332044363483749540)
XLA Ops:
  8.2 2.5 collective-permute-start
  13.3 1.9 collective-permute-done.1
  15.5 6.4 %collective-permute-start.3 = (f32[4,34,1,128]{3,0,2,1:T(4,128)S(1)}, f32[4,34,1,128]{3,0,2,1:T(4,128)S(1)}, u32[]{:S(2)}, u32[]{:S(2)}) collective-permute-start(f32[4,34,1,128]{3,0,2,1:T(4,128)S(1)} %copy.535), channel_id=1, source_target_pairs={{1,0},{2,1},{3,2},{4,3},{5,4},{6,5},{7,6},{8,7},{9,8},{10,9},{11,1... | collective-permute-start | bytes 208904 | tf_op jit(solution)/shard_map/ppermute | solution.py:22
  21.9 2.5 collective-permute-done.2
  33.1 1.5 copy_bitcast_fusion.6
  36.2 1.6 fusion.11
  37.9 17.1 %copy.528 = f32[3,32,16,128]{0,3,2,1:T(8,128)} copy(f32[3,32,16,128]{3,2,1,0:T(8,128)} %fusion.11) | data formatting | bytes 1572864
  54.9 43.8 %gather_fusion = bf16[4096,3]{1,0:T(8,128)(2,1)S(1)} fusion(f32[3,32,16,128]{0,3,2,1:T(8,128)} %copy.528, s32[4096]{0:T(1024)S(1)} %reshape.255), kind=kCustom, calls=%fused_computation | custom fusion | bytes 98304 | tf_op jit(solution)/shard_map/gather | solution.py:101
  102.8 15.8 %all-reduce.2 = (s32[1024]{0:T(1024)S(1)}, s32[1024]{0:T(1024)S(1)}) all-reduce(s32[1024]{0:T(1024)S(1)} %bitcast_dynamic-update-slice_fusion.1, s32[1024]{0:T(1024)S(1)} %bitcast_dynamic-update-slice_fusion), channel_id=3, replica_groups=mesh['gx'=8,'yz'=32] {'yz'}, use_global_device_ids=true, to_apply=%add.1 | all-reduce | flops 2048 | bytes 16384 | tf_op jit(solution)/shard_map/all_gather | solution.py:113
  120.1 3.9 %collective-permute-start.7 = (f32[34,1,128]{2,0,1:T(8,128)S(1)}, f32[34,1,128]{2,0,1:T(8,128)S(1)}, u32[]{:S(2)}, u32[]{:S(2)}) collective-permute-start(f32[34,1,128]{2,0,1:T(8,128)S(1)} %get-tuple-element.71), channel_id=1, source_target_pairs={{1,0},{2,1},{3,2},{4,3},{5,4},{6,5},{7,6},{8,7},{9,8},{10,9},{11,1... | collective-permute-start | bytes 52232 | tf_op jit(solution)/shard_map/ppermute | solution.py:22
  126.3 45.6 %all-gather.4.cloned.1.call-done = f32[1024,384]{1,0:T(8,128)} async-done(((f32[32,384]{1,0:T(8,128)}), f32[1024,384]{1,0:T(8,128)}) %all-gather.4.cloned.1.call-update) | async-done | bytes 1572880 | tf_op jit(solution)/shard_map/all_gather | solution.py:111
  171.9 2.1 fusion
  174.0 36.3 %all_gather.15 = bf16[1024,384]{1,0:T(8,128)(2,1)S(1)} all-gather(bf16[32,384]{1,0:T(8,128)(2,1)S(1)} %fusion), channel_id=1, replica_groups=mesh['gx'=8,'yz'=32] {'yz'}, dimensions={0}, use_global_device_ids=true | all-gather | bytes 811008 | tf_op jit(solution)/shard_map/all_gather | solution.py:122
  211.3 2.0 copy.532
  213.3 42.0 %scatter_fusion = f32[3,65536]{0,1:T(8,128)} fusion(f32[3,65536]{0,1:T(8,128)} %bitcast.96, s32[4096]{0:T(1024)S(1)} %reshape.269, f32[4096,3]{1,0:T(8,128)} %bitcast.106), kind=kCustom, calls=%fused_computation.2 | custom fusion | flops 12288 | bytes 163840
  255.3 20.3 %slice_reduce_fusion = f32[65536]{0:T(1024)S(1)} fusion(f32[3,65536]{0,1:T(8,128)} %scatter_fusion), kind=kLoop, calls=%fused_computation.3 | loop fusion | bytes 524288 | tf_op jit(solution)/shard_map/slice | solution.py:135
  275.6 18.8 %copy.526 = f32[3,32,16,128]{3,2,1,0:T(8,128)S(1)} copy(f32[3,32,16,128]{0,3,2,1:T(8,128)} %bitcast.97) | data formatting | bytes 1572864 | tf_op jit(solution)/shard_map/scatter-add | solution.py:131
  294.4 17.8 %collective-permute-start.8 = (f32[3,1,16,128]{3,2,1,0:T(8,128)S(1)}, f32[3,1,16,128]{3,2,1,0:T(8,128)S(1)}, u32[]{:S(2)}, u32[]{:S(2)}) collective-permute-start(f32[3,1,16,128]{3,2,1,0:T(8,128)S(1)} %get-tuple-element.48), channel_id=1, source_target_pairs={{0,32},{32,64},{64,96},{96,128},{128,160},{160,192},{192,224},{224... | collective-permute-start | bytes 73736 | tf_op jit(solution)/shard_map/ppermute | solution.py:19
  313.2 3.5 collective-permute-done.9
  316.9 4.8 %collective-permute-start.11 = (f32[3,34,1,128]{3,2,1,0:T(1,128)S(1)}, f32[3,34,1,128]{3,2,1,0:T(1,128)S(1)}, u32[]{:S(2)}, u32[]{:S(2)}) collective-permute-start(f32[3,34,1,128]{3,2,1,0:T(1,128)S(1)} %get-tuple-element.47), channel_id=1, source_target_pairs={{1,0},{2,1},{3,2},{4,3},{5,4},{6,5},{7,6},{8,7},{9,8},{10,9},{11,1... | collective-permute-start | bytes 156680 | tf_op jit(solution)/shard_map/ppermute | solution.py:22
  326.7 3.5 collective-permute-done.13
  330.3 5.1 %collective-permute-start.15 = (f32[34,1,128]{2,0,1:T(8,128)S(1)}, f32[34,1,128]{2,0,1:T(8,128)S(1)}, u32[]{:S(2)}, u32[]{:S(2)}) collective-permute-start(f32[34,1,128]{2,0,1:T(8,128)S(1)} %get-tuple-element.69), channel_id=1, source_target_pairs={{1,0},{2,1},{3,2},{4,3},{5,4},{6,5},{7,6},{8,7},{9,8},{10,9},{11,1... | collective-permute-start | bytes 52232 | tf_op jit(solution)/shard_map/ppermute | solution.py:22
  338.9 3.5 collective-permute-done.17
  342.5 5.2 %collective-permute-start.19 = (f32[34,1,128]{2,0,1:T(8,128)S(1)}, f32[34,1,128]{2,0,1:T(8,128)S(1)}, u32[]{:S(2)}, u32[]{:S(2)}) collective-permute-start(f32[34,1,128]{2,0,1:T(8,128)S(1)} %get-tuple-element.67), channel_id=1, source_target_pairs={{1,0},{2,1},{3,2},{4,3},{5,4},{6,5},{7,6},{8,7},{9,8},{10,9},{11,1... | collective-permute-start | bytes 52232 | tf_op jit(solution)/shard_map/ppermute | solution.py:22
  (174 shorter events, 35.8 us)
Async XLA Ops:
  7.2 91.7 %copy-start = (bf16[1,32,128,128]{3,2,1,0:T(8,128)(2,1)S(1)}, bf16[1,32,128,128]{3,2,1,0:T(8,128)(2,1)}, u32[]{:S(2)}) copy-start(bf16[1,32,128,128]{3,2,1,0:T(8,128)(2,1)} %param.9) | copy-start | bytes 3145732
  7.2 164.7 %all-gather.4.cloned.1.call-start = ((), (), s32[]{:S(2)}) async-start(), calls=%async_computation | async-start | bytes 1622016 | tf_op jit(solution)/shard_map/all_gather | solution.py:111
  8.2 5.1 %collective-permute-start = (f32[4,1,16,128]{3,2,1,0:T(8,128)S(1)}, f32[4,1,16,128]{3,2,1,0:T(8,128)S(1)}, u32[]{:S(2)}, u32[]{:S(2)}) collective-permute-start(f32[4,1,16,128]{3,2,1,0:T(8,128)S(1)} %get-tuple-element.44), channel_id=1, source_target_pairs={{0,32},{32,64},{64,96},{96,128},{128,160},{160,192},{192,224},{224... | collective-permute-start | bytes 98312 | tf_op jit(solution)/shard_map/ppermute | solution.py:19
  10.6 4.6 %collective-permute-start.1 = (f32[4,1,16,128]{3,2,1,0:T(8,128)S(1)}, f32[4,1,16,128]{3,2,1,0:T(8,128)S(1)}, u32[]{:S(2)}, u32[]{:S(2)}) collective-permute-start(f32[4,1,16,128]{3,2,1,0:T(8,128)S(1)} %get-tuple-element.45), channel_id=1, source_target_pairs={{32,0},{64,32},{96,64},{128,96},{160,128},{192,160},{224,192},{0,2... | collective-permute-start | bytes 98312 | tf_op jit(solution)/shard_map/ppermute | solution.py:22
  15.3 9.0 %collective-permute-start.2 = (f32[4,34,1,128]{3,0,2,1:T(4,128)S(1)}, f32[4,34,1,128]{3,0,2,1:T(4,128)S(1)}, u32[]{:S(2)}, u32[]{:S(2)}) collective-permute-start(f32[4,34,1,128]{3,0,2,1:T(4,128)S(1)} %copy.534), channel_id=1, source_target_pairs={{0,1},{1,2},{2,3},{3,4},{4,5},{5,6},{6,7},{7,8},{8,9},{9,10},{10,1... | collective-permute-start | bytes 208904 | tf_op jit(solution)/shard_map/ppermute | solution.py:19
  15.5 9.0 %collective-permute-start.3 = (f32[4,34,1,128]{3,0,2,1:T(4,128)S(1)}, f32[4,34,1,128]{3,0,2,1:T(4,128)S(1)}, u32[]{:S(2)}, u32[]{:S(2)}) collective-permute-start(f32[4,34,1,128]{3,0,2,1:T(4,128)S(1)} %copy.535), channel_id=1, source_target_pairs={{1,0},{2,1},{3,2},{4,3},{5,4},{6,5},{7,6},{8,7},{9,8},{10,9},{11,1... | collective-permute-start | bytes 208904 | tf_op jit(solution)/shard_map/ppermute | solution.py:22
  98.8 25.2 %copy-start.14 = (f32[1,32,3,128]{3,1,2,0:T(8,128)S(1)}, f32[1,32,3,128]{3,1,2,0:T(8,128)}, u32[]{:S(2)}) copy-start(f32[1,32,3,128]{3,1,2,0:T(8,128)} %param.10) | copy-start | bytes 147460
  99.5 25.7 %copy-start.17 = (pred[18]{0:T(512)(128)(4,1)S(1)}, pred[18]{0:T(512)(128)(4,1)}, u32[]{:S(2)}) copy-start(pred[18]{0:T(512)(128)(4,1)} %copy-done.16) | copy-start | bytes 58
  100.2 18.9 %collective-permute-start.4 = (f32[1,16,128]{2,0,1:T(1,128)S(1)}, f32[1,16,128]{2,0,1:T(1,128)S(1)}, u32[]{:S(2)}, u32[]{:S(2)}) collective-permute-start(f32[1,16,128]{2,0,1:T(1,128)S(1)} %bitcast.120), channel_id=1, source_target_pairs={{0,32},{32,64},{64,96},{96,128},{128,160},{160,192},{192,224},{224... | collective-permute-start | bytes 24584 | tf_op jit(solution)/shard_map/ppermute | solution.py:19
  101.4 17.7 %collective-permute-start.5 = (f32[1,16,128]{2,0,1:T(1,128)S(1)}, f32[1,16,128]{2,0,1:T(1,128)S(1)}, u32[]{:S(2)}, u32[]{:S(2)}) collective-permute-start(f32[1,16,128]{2,0,1:T(1,128)S(1)} %bitcast.119), channel_id=1, source_target_pairs={{32,0},{64,32},{96,64},{128,96},{160,128},{192,160},{224,192},{0,2... | collective-permute-start | bytes 24584 | tf_op jit(solution)/shard_map/ppermute | solution.py:22
  119.1 6.1 %collective-permute-start.6 = (f32[34,1,128]{2,0,1:T(8,128)S(1)}, f32[34,1,128]{2,0,1:T(8,128)S(1)}, u32[]{:S(2)}, u32[]{:S(2)}) collective-permute-start(f32[34,1,128]{2,0,1:T(8,128)S(1)} %get-tuple-element.70), channel_id=1, source_target_pairs={{0,1},{1,2},{2,3},{3,4},{4,5},{5,6},{6,7},{7,8},{8,9},{9,10},{10,1... | collective-permute-start | bytes 52232 | tf_op jit(solution)/shard_map/ppermute | solution.py:19
  120.1 5.1 %collective-permute-start.7 = (f32[34,1,128]{2,0,1:T(8,128)S(1)}, f32[34,1,128]{2,0,1:T(8,128)S(1)}, u32[]{:S(2)}, u32[]{:S(2)}) collective-permute-start(f32[34,1,128]{2,0,1:T(8,128)S(1)} %get-tuple-element.71), channel_id=1, source_target_pairs={{1,0},{2,1},{3,2},{4,3},{5,4},{6,5},{7,6},{8,7},{9,8},{10,9},{11,1... | collective-permute-start | bytes 52232 | tf_op jit(solution)/shard_map/ppermute | solution.py:22
  294.4 18.8 %collective-permute-start.8 = (f32[3,1,16,128]{3,2,1,0:T(8,128)S(1)}, f32[3,1,16,128]{3,2,1,0:T(8,128)S(1)}, u32[]{:S(2)}, u32[]{:S(2)}) collective-permute-start(f32[3,1,16,128]{3,2,1,0:T(8,128)S(1)} %get-tuple-element.48), channel_id=1, source_target_pairs={{0,32},{32,64},{64,96},{96,128},{128,160},{160,192},{192,224},{224... | collective-permute-start | bytes 73736 | tf_op jit(solution)/shard_map/ppermute | solution.py:19
  312.2 4.5 %collective-permute-start.9 = (f32[3,1,16,128]{3,2,1,0:T(8,128)S(1)}, f32[3,1,16,128]{3,2,1,0:T(8,128)S(1)}, u32[]{:S(2)}, u32[]{:S(2)}) collective-permute-start(f32[3,1,16,128]{3,2,1,0:T(8,128)S(1)} %get-tuple-element.49), channel_id=1, source_target_pairs={{32,0},{64,32},{96,64},{128,96},{160,128},{192,160},{224,192},{0,2... | collective-permute-start | bytes 73736 | tf_op jit(solution)/shard_map/ppermute | solution.py:22
  316.8 6.4 %collective-permute-start.10 = (f32[3,34,1,128]{3,2,1,0:T(1,128)S(1)}, f32[3,34,1,128]{3,2,1,0:T(1,128)S(1)}, u32[]{:S(2)}, u32[]{:S(2)}) collective-permute-start(f32[3,34,1,128]{3,2,1,0:T(1,128)S(1)} %get-tuple-element.46), channel_id=1, source_target_pairs={{0,1},{1,2},{2,3},{3,4},{4,5},{5,6},{6,7},{7,8},{8,9},{9,10},{10,1... | collective-permute-start | bytes 156680 | tf_op jit(solution)/shard_map/ppermute | solution.py:19
  316.9 6.3 %collective-permute-start.11 = (f32[3,34,1,128]{3,2,1,0:T(1,128)S(1)}, f32[3,34,1,128]{3,2,1,0:T(1,128)S(1)}, u32[]{:S(2)}, u32[]{:S(2)}) collective-permute-start(f32[3,34,1,128]{3,2,1,0:T(1,128)S(1)} %get-tuple-element.47), channel_id=1, source_target_pairs={{1,0},{2,1},{3,2},{4,3},{5,4},{6,5},{7,6},{8,7},{9,8},{10,9},{11,1... | collective-permute-start | bytes 156680 | tf_op jit(solution)/shard_map/ppermute | solution.py:22
  324.8 2.0 collective-permute-start.12
  325.9 4.3 %collective-permute-start.13 = (f32[1,16,128]{2,0,1:T(1,128)S(1)}, f32[1,16,128]{2,0,1:T(1,128)S(1)}, u32[]{:S(2)}, u32[]{:S(2)}) collective-permute-start(f32[1,16,128]{2,0,1:T(1,128)S(1)} %get-tuple-element.75), channel_id=1, source_target_pairs={{32,0},{64,32},{96,64},{128,96},{160,128},{192,160},{224,192},{0,2... | collective-permute-start | bytes 24584 | tf_op jit(solution)/shard_map/ppermute | solution.py:22
  330.2 6.3 %collective-permute-start.14 = (f32[34,1,128]{2,0,1:T(8,128)S(1)}, f32[34,1,128]{2,0,1:T(8,128)S(1)}, u32[]{:S(2)}, u32[]{:S(2)}) collective-permute-start(f32[34,1,128]{2,0,1:T(8,128)S(1)} %get-tuple-element.68), channel_id=1, source_target_pairs={{0,1},{1,2},{2,3},{3,4},{4,5},{5,6},{6,7},{7,8},{8,9},{9,10},{10,1... | collective-permute-start | bytes 52232 | tf_op jit(solution)/shard_map/ppermute | solution.py:19
  330.3 6.2 %collective-permute-start.15 = (f32[34,1,128]{2,0,1:T(8,128)S(1)}, f32[34,1,128]{2,0,1:T(8,128)S(1)}, u32[]{:S(2)}, u32[]{:S(2)}) collective-permute-start(f32[34,1,128]{2,0,1:T(8,128)S(1)} %get-tuple-element.69), channel_id=1, source_target_pairs={{1,0},{2,1},{3,2},{4,3},{5,4},{6,5},{7,6},{8,7},{9,8},{10,9},{11,1... | collective-permute-start | bytes 52232 | tf_op jit(solution)/shard_map/ppermute | solution.py:22
  337.2 1.7 collective-permute-start.16
  338.1 4.3 %collective-permute-start.17 = (f32[1,16,128]{2,0,1:T(1,128)S(1)}, f32[1,16,128]{2,0,1:T(1,128)S(1)}, u32[]{:S(2)}, u32[]{:S(2)}) collective-permute-start(f32[1,16,128]{2,0,1:T(1,128)S(1)} %get-tuple-element.73), channel_id=1, source_target_pairs={{32,0},{64,32},{96,64},{128,96},{160,128},{192,160},{224,192},{0,2... | collective-permute-start | bytes 24584 | tf_op jit(solution)/shard_map/ppermute | solution.py:22
  342.4 6.4 %collective-permute-start.18 = (f32[34,1,128]{2,0,1:T(8,128)S(1)}, f32[34,1,128]{2,0,1:T(8,128)S(1)}, u32[]{:S(2)}, u32[]{:S(2)}) collective-permute-start(f32[34,1,128]{2,0,1:T(8,128)S(1)} %get-tuple-element.66), channel_id=1, source_target_pairs={{0,1},{1,2},{2,3},{3,4},{4,5},{5,6},{6,7},{7,8},{8,9},{9,10},{10,1... | collective-permute-start | bytes 52232 | tf_op jit(solution)/shard_map/ppermute | solution.py:19
  342.5 6.3 %collective-permute-start.19 = (f32[34,1,128]{2,0,1:T(8,128)S(1)}, f32[34,1,128]{2,0,1:T(8,128)S(1)}, u32[]{:S(2)}, u32[]{:S(2)}) collective-permute-start(f32[34,1,128]{2,0,1:T(8,128)S(1)} %get-tuple-element.67), channel_id=1, source_target_pairs={{1,0},{2,1},{3,2},{4,3},{5,4},{6,5},{7,6},{8,7},{9,8},{10,9},{11,1... | collective-permute-start | bytes 52232 | tf_op jit(solution)/shard_map/ppermute | solution.py:22
  (22 other events, 162.0 us)
Sparse Core Ops, SparseCore 0:
  100.3 71.5 all-gather.3
where the time goes:
time: 360 us; the launch traced here: 359 us
  local copies, waits for them, and re-layouts  120 us (33%)
  waiting for transfers between devices  65.7 us (18%)
  blocking collectives  52.1 us (14%)
  other arithmetic  51.9 us (14%)
  starting transfers between devices  50.3 us (14%)
  between operations  15.5 us (4%)
    all_gather x1, waiting for transfers between devices, body(): lax.all_gather(flat_partial, 'yz', axis=0, tiled=True)  45.6 us
    gather x1, local copies, waits for them, and re-layouts, body(): predicted[:, cell_x, cell_z, cell_y].astype(jnp.bfloat16)  43.8 us
    unnamed x4, other arithmetic  42.2 us
    all_gather x1, blocking collectives, body(): all_force = lax.all_gather(grain_force, 'yz', axis=0, tiled=True)  36.3 us
    ppermute x10, starting transfers between devices, extended(): lax.ppermute(lax.slice_in_dim(block, 0, width, axis=dim), axis, backward)  25.4 us
    ppermute x10, starting transfers between devices, extended(): lax.ppermute(lax.slice_in_dim(block, block.shape[dim] - width, None, axis...  24.9 us
    unnamed x69, local copies, waits for them, and re-layouts  22 us
    slice x1, local copies, waits for them, and re-layouts, body(): forced_velocity[1]  20.3 us
  transfers between devices with their start and end apart: 21, of which 13 were waited for; matrix products, arithmetic and copies ran while one was open for 2% of the time, Pallas kernels for 0%

commit v1 on v0

--- a/solution.py
+++ b/solution.py
@@ -108,7 +108,9 @@
     targets = marker_target[0].reshape(grain_slots, row_width)
     slot_numbers = jnp.arange(grain_slots, dtype=jnp.int32)
     all_partial, all_owner, all_grain = (
-        lax.all_gather(flat_partial, "yz", axis=0, tiled=True),
+        jnp.concatenate(
+            lax.all_to_all(jnp.stack(lax.axis_size("yz") * [flat_partial], axis=0), "yz", 0, 0), 0
+        ),
         lax.all_gather(owners, "yz", axis=0, tiled=True),
         lax.all_gather(grains, "yz", axis=0, tiled=True),
     )

time: 360 us -> 331 us (0.919)
  waiting for transfers between devices: 65.7 us -> 19.3 us
  blocking collectives: 52.1 us -> 75.9 us
  between operations: 15.5 us -> 2.03 us
  starting transfers between devices: 50.3 us -> 56.8 us
    all_gather x1 -> x0, waiting for transfers between devices: 45.6 us -> none  [body(): lax.all_gather(flat_partial, 'yz', axis=0, tiled=True)]
    all_gather x1, blocking collectives: 15.8 us -> 38.2 us  [body(): lax.all_gather(grains, 'yz', axis=0, tiled=True)]
    all_to_all x0 -> x1, starting transfers between devices: none -> 7.62 us  [body(): lax.all_to_all(jnp.stack(lax.axis_size('yz') * [flat_partial], axis=0), '...]
  transfers between devices with their start and end apart: 21 -> 21, of which waited for: 13 -> 12; matrix products, arithmetic and copies ran while one was open for 2% -> 2% of each run, Pallas kernels for 0% -> 0%
where the time goes in v1:
time: 331 us; the launch traced here: 330 us
  local copies, waits for them, and re-layouts  122 us (37%)
  blocking collectives  75.9 us (23%)
  starting transfers between devices  56.8 us (17%)
  other arithmetic  51.9 us (16%)
  waiting for transfers between devices  19.3 us (6%)
    gather x1, local copies, waits for them, and re-layouts, body(): predicted[:, cell_x, cell_z, cell_y].astype(jnp.bfloat16)  43.8 us
    unnamed x4, other arithmetic  42.2 us
    all_gather x1, blocking collectives, body(): lax.all_gather(grains, 'yz', axis=0, tiled=True)  38.2 us
    all_gather x1, blocking collectives, body(): all_force = lax.all_gather(grain_force, 'yz', axis=0, tiled=True)  37.7 us
    ppermute x10, starting transfers between devices, extended(): lax.ppermute(lax.slice_in_dim(block, 0, width, axis=dim), axis, backward)  25.4 us
    ppermute x10, starting transfers between devices, extended(): lax.ppermute(lax.slice_in_dim(block, block.shape[dim] - width, None, axis...  23.8 us
    unnamed x69, local copies, waits for them, and re-layouts  22 us
    slice x1, local copies, waits for them, and re-layouts, body(): forced_velocity[1]  20.3 us
  transfers between devices with their start and end apart: 21, of which 12 were waited for; matrix products, arithmetic and copies ran while one was open for 2% of the time, Pallas kernels for 0%

profile of v1, /device:TPU:7, one launch (start us, length us, event | category | flops | bytes accessed | tf_op | source)
XLA Modules:
  0.0 330.0 jit_solution(365592588748647591)
XLA Ops:
  1.6 2.5 collective-permute-start
  6.7 1.9 collective-permute-done.1
  8.9 6.4 %collective-permute-start.3 = (f32[4,34,1,128]{3,0,2,1:T(4,128)S(1)}, f32[4,34,1,128]{3,0,2,1:T(4,128)S(1)}, u32[]{:S(2)}, u32[]{:S(2)}) collective-permute-start(f32[4,34,1,128]{3,0,2,1:T(4,128)S(1)} %copy.535), channel_id=1, source_target_pairs={{1,0},{2,1},{3,2},{4,3},{5,4},{6,5},{7,6},{8,7},{9,8},{10,9},{11,1... | collective-permute-start | bytes 208904 | tf_op jit(solution)/shard_map/ppermute | solution.py:22
  15.3 2.5 collective-permute-done.2
  29.7 1.6 fusion.11
  31.3 17.1 %copy.528 = f32[3,32,16,128]{0,3,2,1:T(8,128)} copy(f32[3,32,16,128]{3,2,1,0:T(8,128)} %fusion.11) | data formatting | bytes 1572864
  48.5 43.8 %gather_fusion = bf16[4096,3]{1,0:T(8,128)(2,1)S(1)} fusion(f32[3,32,16,128]{0,3,2,1:T(8,128)} %copy.528, s32[4096]{0:T(1024)S(1)} %reshape.257), kind=kCustom, calls=%fused_computation | custom fusion | bytes 98304 | tf_op jit(solution)/shard_map/gather | solution.py:101
  94.4 7.6 %all-to-all-start = ((f32[32,32,384]{2,1,0:T(8,128)}), f32[32,32,384]{2,1,0:T(8,128)S(1)}, u32[]{:S(2)}, u32[]{:S(2)}) async-start(f32[32,32,384]{2,1,0:T(8,128)} %stack.26), calls=%async_computation | async-start | bytes 3145728 | tf_op jit(solution)/shard_map/all_to_all | solution.py:112
  102.1 2.2 collective-permute-start.4
  105.7 38.2 %all-reduce.2 = (s32[1024]{0:T(1024)S(1)}, s32[1024]{0:T(1024)S(1)}) all-reduce(s32[1024]{0:T(1024)S(1)} %bitcast_dynamic-update-slice_fusion.1, s32[1024]{0:T(1024)S(1)} %bitcast_dynamic-update-slice_fusion), channel_id=3, replica_groups=mesh['gx'=8,'yz'=32] {'yz'}, use_global_device_ids=true, to_apply=%add.1 | all-reduce | flops 2048 | bytes 16384 | tf_op jit(solution)/shard_map/all_gather | solution.py:115
  145.6 3.6 %collective-permute-start.7 = (f32[34,1,128]{2,0,1:T(8,128)S(1)}, f32[34,1,128]{2,0,1:T(8,128)S(1)}, u32[]{:S(2)}, u32[]{:S(2)}) collective-permute-start(f32[34,1,128]{2,0,1:T(8,128)S(1)} %get-tuple-element.71), channel_id=1, source_target_pairs={{1,0},{2,1},{3,2},{4,3},{5,4},{6,5},{7,6},{8,7},{9,8},{10,9},{11,1... | collective-permute-start | bytes 52232 | tf_op jit(solution)/shard_map/ppermute | solution.py:22
  151.5 1.5 fusion
  153.1 37.7 %all_gather.11 = bf16[1024,384]{1,0:T(8,128)(2,1)S(1)} all-gather(bf16[32,384]{1,0:T(8,128)(2,1)S(1)} %fusion), channel_id=1, replica_groups=mesh['gx'=8,'yz'=32] {'yz'}, dimensions={0}, use_global_device_ids=true | all-gather | bytes 811008 | tf_op jit(solution)/shard_map/all_gather | solution.py:124
  191.8 2.0 copy.532
  193.8 42.0 %scatter_fusion = f32[3,65536]{0,1:T(8,128)} fusion(f32[3,65536]{0,1:T(8,128)} %bitcast.97, s32[4096]{0:T(1024)S(1)} %reshape.271, f32[4096,3]{1,0:T(8,128)} %bitcast.108), kind=kCustom, calls=%fused_computation.2 | custom fusion | flops 12288 | bytes 163840
  235.8 20.3 %slice_reduce_fusion = f32[65536]{0:T(1024)S(1)} fusion(f32[3,65536]{0,1:T(8,128)} %scatter_fusion), kind=kLoop, calls=%fused_computation.3 | loop fusion | bytes 524288 | tf_op jit(solution)/shard_map/slice | solution.py:137
  256.1 18.8 %copy.526 = f32[3,32,16,128]{3,2,1,0:T(8,128)S(1)} copy(f32[3,32,16,128]{0,3,2,1:T(8,128)} %bitcast.98) | data formatting | bytes 1572864 | tf_op jit(solution)/shard_map/scatter-add | solution.py:133
  274.9 14.9 %collective-permute-start.8 = (f32[3,1,16,128]{3,2,1,0:T(8,128)S(1)}, f32[3,1,16,128]{3,2,1,0:T(8,128)S(1)}, u32[]{:S(2)}, u32[]{:S(2)}) collective-permute-start(f32[3,1,16,128]{3,2,1,0:T(8,128)S(1)} %get-tuple-element.48), channel_id=1, source_target_pairs={{0,32},{32,64},{64,96},{96,128},{128,160},{160,192},{192,224},{224... | collective-permute-start | bytes 73736 | tf_op jit(solution)/shard_map/ppermute | solution.py:19
  291.3 3.0 collective-permute-done.9
  295.6 3.7 %collective-permute-start.11 = (f32[3,34,1,128]{3,2,1,0:T(1,128)S(1)}, f32[3,34,1,128]{3,2,1,0:T(1,128)S(1)}, u32[]{:S(2)}, u32[]{:S(2)}) collective-permute-start(f32[3,34,1,128]{3,2,1,0:T(1,128)S(1)} %get-tuple-element.47), channel_id=1, source_target_pairs={{1,0},{2,1},{3,2},{4,3},{5,4},{6,5},{7,6},{8,7},{9,8},{10,9},{11,1... | collective-permute-start | bytes 156680 | tf_op jit(solution)/shard_map/ppermute | solution.py:22
  304.7 3.5 %collective-permute-done.13 = f32[1,16,128]{2,0,1:T(1,128)S(1)} collective-permute-done((f32[1,16,128]{2,0,1:T(1,128)S(1)}, f32[1,16,128]{2,0,1:T(1,128)S(1)}, u32[]{:S(2)}, u32[]{:S(2)}) %collective-permute-start.13) | collective-permute-done | bytes 8224 | tf_op jit(solution)/shard_map/ppermute | solution.py:22
  308.3 5.4 %collective-permute-start.15 = (f32[34,1,128]{2,0,1:T(8,128)S(1)}, f32[34,1,128]{2,0,1:T(8,128)S(1)}, u32[]{:S(2)}, u32[]{:S(2)}) collective-permute-start(f32[34,1,128]{2,0,1:T(8,128)S(1)} %get-tuple-element.69), channel_id=1, source_target_pairs={{1,0},{2,1},{3,2},{4,3},{5,4},{6,5},{7,6},{8,7},{9,8},{10,9},{11,1... | collective-permute-start | bytes 52232 | tf_op jit(solution)/shard_map/ppermute | solution.py:22
  317.0 3.5 %collective-permute-done.17 = f32[1,16,128]{2,0,1:T(1,128)S(1)} collective-permute-done((f32[1,16,128]{2,0,1:T(1,128)S(1)}, f32[1,16,128]{2,0,1:T(1,128)S(1)}, u32[]{:S(2)}, u32[]{:S(2)}) %collective-permute-start.17) | collective-permute-done | bytes 8224 | tf_op jit(solution)/shard_map/ppermute | solution.py:22
  320.6 5.4 %collective-permute-start.19 = (f32[34,1,128]{2,0,1:T(8,128)S(1)}, f32[34,1,128]{2,0,1:T(8,128)S(1)}, u32[]{:S(2)}, u32[]{:S(2)}) collective-permute-start(f32[34,1,128]{2,0,1:T(8,128)S(1)} %get-tuple-element.67), channel_id=1, source_target_pairs={{1,0},{2,1},{3,2},{4,3},{5,4},{6,5},{7,6},{8,7},{9,8},{10,9},{11,1... | collective-permute-start | bytes 52232 | tf_op jit(solution)/shard_map/ppermute | solution.py:22
  (174 shorter events, 38.8 us)
Async XLA Ops:
  0.6 91.7 %copy-start = (bf16[1,32,128,128]{3,2,1,0:T(8,128)(2,1)S(1)}, bf16[1,32,128,128]{3,2,1,0:T(8,128)(2,1)}, u32[]{:S(2)}) copy-start(bf16[1,32,128,128]{3,2,1,0:T(8,128)(2,1)} %param.9) | copy-start | bytes 3145732
  1.6 5.1 %collective-permute-start = (f32[4,1,16,128]{3,2,1,0:T(8,128)S(1)}, f32[4,1,16,128]{3,2,1,0:T(8,128)S(1)}, u32[]{:S(2)}, u32[]{:S(2)}) collective-permute-start(f32[4,1,16,128]{3,2,1,0:T(8,128)S(1)} %get-tuple-element.44), channel_id=1, source_target_pairs={{0,32},{32,64},{64,96},{96,128},{128,160},{160,192},{192,224},{224... | collective-permute-start | bytes 98312 | tf_op jit(solution)/shard_map/ppermute | solution.py:19
  4.1 4.6 %collective-permute-start.1 = (f32[4,1,16,128]{3,2,1,0:T(8,128)S(1)}, f32[4,1,16,128]{3,2,1,0:T(8,128)S(1)}, u32[]{:S(2)}, u32[]{:S(2)}) collective-permute-start(f32[4,1,16,128]{3,2,1,0:T(8,128)S(1)} %get-tuple-element.45), channel_id=1, source_target_pairs={{32,0},{64,32},{96,64},{128,96},{160,128},{192,160},{224,192},{0,2... | collective-permute-start | bytes 98312 | tf_op jit(solution)/shard_map/ppermute | solution.py:22
  8.8 9.0 %collective-permute-start.2 = (f32[4,34,1,128]{3,0,2,1:T(4,128)S(1)}, f32[4,34,1,128]{3,0,2,1:T(4,128)S(1)}, u32[]{:S(2)}, u32[]{:S(2)}) collective-permute-start(f32[4,34,1,128]{3,0,2,1:T(4,128)S(1)} %copy.534), channel_id=1, source_target_pairs={{0,1},{1,2},{2,3},{3,4},{4,5},{5,6},{6,7},{7,8},{8,9},{9,10},{10,1... | collective-permute-start | bytes 208904 | tf_op jit(solution)/shard_map/ppermute | solution.py:19
  8.9 9.0 %collective-permute-start.3 = (f32[4,34,1,128]{3,0,2,1:T(4,128)S(1)}, f32[4,34,1,128]{3,0,2,1:T(4,128)S(1)}, u32[]{:S(2)}, u32[]{:S(2)}) collective-permute-start(f32[4,34,1,128]{3,0,2,1:T(4,128)S(1)} %copy.535), channel_id=1, source_target_pairs={{1,0},{2,1},{3,2},{4,3},{5,4},{6,5},{7,6},{8,7},{9,8},{10,9},{11,1... | collective-permute-start | bytes 208904 | tf_op jit(solution)/shard_map/ppermute | solution.py:22
  94.4 49.6 %copy-start.21 = (s32[3]{0:T(128)S(1)}, s32[3]{0:T(128)}, u32[]{:S(2)}) copy-start(s32[3]{0:T(128)} %constant.64) | copy-start | bytes 40
  94.4 49.7 %copy-start.20 = (s32[3]{0:T(128)S(1)}, s32[3]{0:T(128)}, u32[]{:S(2)}) copy-start(s32[3]{0:T(128)} %constant.67) | copy-start | bytes 40
  94.4 57.1 %all-to-all-start = ((f32[32,32,384]{2,1,0:T(8,128)}), f32[32,32,384]{2,1,0:T(8,128)S(1)}, u32[]{:S(2)}, u32[]{:S(2)}) async-start(f32[32,32,384]{2,1,0:T(8,128)} %stack.26), calls=%async_computation | async-start | bytes 3145728 | tf_op jit(solution)/shard_map/all_to_all | solution.py:112
  102.1 42.3 %collective-permute-start.4 = (f32[1,16,128]{2,0,1:T(1,128)S(1)}, f32[1,16,128]{2,0,1:T(1,128)S(1)}, u32[]{:S(2)}, u32[]{:S(2)}) collective-permute-start(f32[1,16,128]{2,0,1:T(1,128)S(1)} %bitcast.122), channel_id=1, source_target_pairs={{0,32},{32,64},{64,96},{96,128},{128,160},{160,192},{192,224},{224... | collective-permute-start | bytes 24584 | tf_op jit(solution)/shard_map/ppermute | solution.py:19
  104.2 40.1 %collective-permute-start.5 = (f32[1,16,128]{2,0,1:T(1,128)S(1)}, f32[1,16,128]{2,0,1:T(1,128)S(1)}, u32[]{:S(2)}, u32[]{:S(2)}) collective-permute-start(f32[1,16,128]{2,0,1:T(1,128)S(1)} %bitcast.121), channel_id=1, source_target_pairs={{32,0},{64,32},{96,64},{128,96},{160,128},{192,160},{224,192},{0,2... | collective-permute-start | bytes 24584 | tf_op jit(solution)/shard_map/ppermute | solution.py:22
  144.4 6.0 %collective-permute-start.6 = (f32[34,1,128]{2,0,1:T(8,128)S(1)}, f32[34,1,128]{2,0,1:T(8,128)S(1)}, u32[]{:S(2)}, u32[]{:S(2)}) collective-permute-start(f32[34,1,128]{2,0,1:T(8,128)S(1)} %get-tuple-element.70), channel_id=1, source_target_pairs={{0,1},{1,2},{2,3},{3,4},{4,5},{5,6},{6,7},{7,8},{8,9},{9,10},{10,1... | collective-permute-start | bytes 52232 | tf_op jit(solution)/shard_map/ppermute | solution.py:19
  145.6 4.8 %collective-permute-start.7 = (f32[34,1,128]{2,0,1:T(8,128)S(1)}, f32[34,1,128]{2,0,1:T(8,128)S(1)}, u32[]{:S(2)}, u32[]{:S(2)}) collective-permute-start(f32[34,1,128]{2,0,1:T(8,128)S(1)} %get-tuple-element.71), channel_id=1, source_target_pairs={{1,0},{2,1},{3,2},{4,3},{5,4},{6,5},{7,6},{8,7},{9,8},{10,9},{11,1... | collective-permute-start | bytes 52232 | tf_op jit(solution)/shard_map/ppermute | solution.py:22
  274.9 16.4 %collective-permute-start.8 = (f32[3,1,16,128]{3,2,1,0:T(8,128)S(1)}, f32[3,1,16,128]{3,2,1,0:T(8,128)S(1)}, u32[]{:S(2)}, u32[]{:S(2)}) collective-permute-start(f32[3,1,16,128]{3,2,1,0:T(8,128)S(1)} %get-tuple-element.48), channel_id=1, source_target_pairs={{0,32},{32,64},{64,96},{96,128},{128,160},{160,192},{192,224},{224... | collective-permute-start | bytes 73736 | tf_op jit(solution)/shard_map/ppermute | solution.py:19
  289.8 4.5 %collective-permute-start.9 = (f32[3,1,16,128]{3,2,1,0:T(8,128)S(1)}, f32[3,1,16,128]{3,2,1,0:T(8,128)S(1)}, u32[]{:S(2)}, u32[]{:S(2)}) collective-permute-start(f32[3,1,16,128]{3,2,1,0:T(8,128)S(1)} %get-tuple-element.49), channel_id=1, source_target_pairs={{32,0},{64,32},{96,64},{128,96},{160,128},{192,160},{224,192},{0,2... | collective-permute-start | bytes 73736 | tf_op jit(solution)/shard_map/ppermute | solution.py:22
  294.4 7.2 %collective-permute-start.10 = (f32[3,34,1,128]{3,2,1,0:T(1,128)S(1)}, f32[3,34,1,128]{3,2,1,0:T(1,128)S(1)}, u32[]{:S(2)}, u32[]{:S(2)}) collective-permute-start(f32[3,34,1,128]{3,2,1,0:T(1,128)S(1)} %get-tuple-element.46), channel_id=1, source_target_pairs={{0,1},{1,2},{2,3},{3,4},{4,5},{5,6},{6,7},{7,8},{8,9},{9,10},{10,1... | collective-permute-start | bytes 156680 | tf_op jit(solution)/shard_map/ppermute | solution.py:19
  295.6 6.0 %collective-permute-start.11 = (f32[3,34,1,128]{3,2,1,0:T(1,128)S(1)}, f32[3,34,1,128]{3,2,1,0:T(1,128)S(1)}, u32[]{:S(2)}, u32[]{:S(2)}) collective-permute-start(f32[3,34,1,128]{3,2,1,0:T(1,128)S(1)} %get-tuple-element.47), channel_id=1, source_target_pairs={{1,0},{2,1},{3,2},{4,3},{5,4},{6,5},{7,6},{8,7},{9,8},{10,9},{11,1... | collective-permute-start | bytes 156680 | tf_op jit(solution)/shard_map/ppermute | solution.py:22
  303.2 1.5 collective-permute-start.12
  303.9 4.3 %collective-permute-start.13 = (f32[1,16,128]{2,0,1:T(1,128)S(1)}, f32[1,16,128]{2,0,1:T(1,128)S(1)}, u32[]{:S(2)}, u32[]{:S(2)}) collective-permute-start(f32[1,16,128]{2,0,1:T(1,128)S(1)} %get-tuple-element.75), channel_id=1, source_target_pairs={{32,0},{64,32},{96,64},{128,96},{160,128},{192,160},{224,192},{0,2... | collective-permute-start | bytes 24584 | tf_op jit(solution)/shard_map/ppermute | solution.py:22
  308.2 6.4 %collective-permute-start.14 = (f32[34,1,128]{2,0,1:T(8,128)S(1)}, f32[34,1,128]{2,0,1:T(8,128)S(1)}, u32[]{:S(2)}, u32[]{:S(2)}) collective-permute-start(f32[34,1,128]{2,0,1:T(8,128)S(1)} %get-tuple-element.68), channel_id=1, source_target_pairs={{0,1},{1,2},{2,3},{3,4},{4,5},{5,6},{6,7},{7,8},{8,9},{9,10},{10,1... | collective-permute-start | bytes 52232 | tf_op jit(solution)/shard_map/ppermute | solution.py:19
  308.3 6.4 %collective-permute-start.15 = (f32[34,1,128]{2,0,1:T(8,128)S(1)}, f32[34,1,128]{2,0,1:T(8,128)S(1)}, u32[]{:S(2)}, u32[]{:S(2)}) collective-permute-start(f32[34,1,128]{2,0,1:T(8,128)S(1)} %get-tuple-element.69), channel_id=1, source_target_pairs={{1,0},{2,1},{3,2},{4,3},{5,4},{6,5},{7,6},{8,7},{9,8},{10,9},{11,1... | collective-permute-start | bytes 52232 | tf_op jit(solution)/shard_map/ppermute | solution.py:22
  315.3 1.7 collective-permute-start.16
  316.2 4.3 %collective-permute-start.17 = (f32[1,16,128]{2,0,1:T(1,128)S(1)}, f32[1,16,128]{2,0,1:T(1,128)S(1)}, u32[]{:S(2)}, u32[]{:S(2)}) collective-permute-start(f32[1,16,128]{2,0,1:T(1,128)S(1)} %get-tuple-element.73), channel_id=1, source_target_pairs={{32,0},{64,32},{96,64},{128,96},{160,128},{192,160},{224,192},{0,2... | collective-permute-start | bytes 24584 | tf_op jit(solution)/shard_map/ppermute | solution.py:22
  320.5 6.6 %collective-permute-start.18 = (f32[34,1,128]{2,0,1:T(8,128)S(1)}, f32[34,1,128]{2,0,1:T(8,128)S(1)}, u32[]{:S(2)}, u32[]{:S(2)}) collective-permute-start(f32[34,1,128]{2,0,1:T(8,128)S(1)} %get-tuple-element.66), channel_id=1, source_target_pairs={{0,1},{1,2},{2,3},{3,4},{4,5},{5,6},{6,7},{7,8},{8,9},{9,10},{10,1... | collective-permute-start | bytes 52232 | tf_op jit(solution)/shard_map/ppermute | solution.py:19
  320.6 6.5 %collective-permute-start.19 = (f32[34,1,128]{2,0,1:T(8,128)S(1)}, f32[34,1,128]{2,0,1:T(8,128)S(1)}, u32[]{:S(2)}, u32[]{:S(2)}) collective-permute-start(f32[34,1,128]{2,0,1:T(8,128)S(1)} %get-tuple-element.67), channel_id=1, source_target_pairs={{1,0},{2,1},{3,2},{4,3},{5,4},{6,5},{7,6},{8,7},{9,8},{10,9},{11,1... | collective-permute-start | bytes 52232 | tf_op jit(solution)/shard_map/ppermute | solution.py:22
  (22 other events, 334.7 us)
